TPU v7x, 512 devices: a whole 4x8x8 slice. The times are simulated.
512 devices in a mesh: dp: 16 (over y, core), expert: 32 (over x, z).
Axes of the slice: x: 4, y: 8, z: 8, core: 2. Of those that a mesh axis runs over, the one named last changes fastest.
Arguments:
- tokens: bfloat16 [65536, 1024], P(('dp', 'expert')), may hold values from -6 to 6
- routes: int32 [65536, 4], P(('dp', 'expert')), may hold values from 0 to 31, all different within a row; in each aligned block of 128 rows (0 to 127, 128 to 255, ...) at most 32 rows name the same one
- gates: float32 [65536, 4], P(('dp', 'expert')), may hold values from 0.05 to 0.5
- w_in: bfloat16 [32, 1024, 768], P('expert', 'dp'), may hold values from -6 to 6
- w_down: bfloat16 [32, 384, 1024], P('expert', 'dp'), may hold values from -6 to 6
- out_grad: bfloat16 [65536, 1024], P(('dp', 'expert')), may hold values from -6 to 6
Outputs:
- moe_out: bfloat16 [65536, 1024], P(('dp', 'expert'))
- token_grad: bfloat16 [65536, 1024], P(('dp', 'expert'))
- new_w_in: bfloat16 [32, 1024, 768], P('expert', 'dp')
- new_w_down: bfloat16 [32, 384, 1024], P('expert', 'dp')
Inputs may be any that keep to these rules, and one draw needn't show every extreme that they name: `routes`: within one device's 128 tokens no expert is named more than 32 times, a bound that some block reaches; a token names 4 different experts.
All inputs are finite; a program needn't handle non-finite values.
Results may differ from a plain program's by a relative error of at most 0.014.
Values may be sent and summed in bfloat16 or wider, within the bound.
No kernel may reach another device: no remote copies, remote signals or barrier semaphores. Data moves between devices by JAX's collectives and lax.ppermute only.
A program may use at most 64 MiB of HBM per device.

v0:
```python
import jax
import jax.numpy as jnp
from jax import lax
from jax.sharding import PartitionSpec as P

step_rate = 0.5


def slot_numbers(route_rows, experts, capacity):
    flat_routes = route_rows.reshape(-1)
    one_hot = (flat_routes[:, None] == jnp.arange(experts, dtype=jnp.int32)[None, :]).astype(
        jnp.int32
    )
    running = jnp.cumsum(one_hot, axis=0)
    position = jnp.sum(one_hot * running, axis=1) - 1
    return flat_routes * capacity + position


def expert_forward(inputs, full_in, full_down):
    model_width = full_in.shape[1]
    hidden_units = full_down.shape[1]
    projected = jnp.einsum(
        "sxcd,xdj->sxcj", inputs, full_in, preferred_element_type=jnp.float32
    ) * model_width ** (-0.5)
    gate_part = projected[..., :hidden_units]
    up_part = projected[..., hidden_units:]
    activation = (jax.nn.silu(gate_part) * up_part).astype(jnp.bfloat16)
    results = (
        jnp.einsum("sxcf,xfd->sxcd", activation, full_down, preferred_element_type=jnp.float32)
        * hidden_units ** (-0.5)
    ).astype(jnp.bfloat16)
    return (projected, activation, results)


def expert_backward(projected, grad_rows, full_in, full_down):
    model_width = full_in.shape[1]
    hidden_units = full_down.shape[1]
    grad_act = jnp.einsum(
        "sxcd,xfd->sxcf", grad_rows, full_down, preferred_element_type=jnp.float32
    ) * hidden_units ** (-0.5)
    gate_part = projected[..., :hidden_units]
    up_part = projected[..., hidden_units:]
    sigmoid_gate = jax.nn.sigmoid(gate_part)
    grad_gate = grad_act * up_part * sigmoid_gate * (1.0 + gate_part * (1.0 - sigmoid_gate))
    grad_up = grad_act * jax.nn.silu(gate_part)
    grad_hidden = jnp.concatenate([grad_gate, grad_up], axis=-1).astype(jnp.bfloat16)
    grad_inputs = (
        jnp.einsum("sxcj,xdj->sxcd", grad_hidden, full_in, preferred_element_type=jnp.float32)
        * model_width ** (-0.5)
    ).astype(jnp.bfloat16)
    return (grad_hidden, grad_inputs)


def body(tokens, routes, gates, w_in, w_down, out_grad):
    tok_rows, model_width = tokens.shape
    top_count = routes.shape[1]
    per_device = w_in.shape[0]
    hidden_units = w_down.shape[2] and w_in.shape[2] // 2
    sources = lax.axis_size("expert")
    experts = per_device * sources
    capacity = min(tok_rows, 2 * tok_rows * top_count // experts)
    slot_index = slot_numbers(routes, experts, capacity)
    token_of = jnp.arange(tok_rows * top_count, dtype=jnp.int32) // top_count
    layout = (sources, per_device, capacity, model_width)
    send_inputs = (
        jnp.zeros((experts * capacity, model_width), jnp.bfloat16)
        .at[slot_index]
        .set(tokens[token_of])
        .reshape(layout)
    )
    scaled = (gates.reshape(-1)[:, None] * out_grad[token_of].astype(jnp.float32)).astype(
        jnp.bfloat16
    )
    send_grads = (
        jnp.zeros((experts * capacity, model_width), jnp.bfloat16)
        .at[slot_index]
        .set(scaled)
        .reshape(layout)
    )
    full_in, full_down = (
        lax.all_gather(w_in, "dp", axis=1, tiled=True),
        lax.all_gather(w_down, "dp", axis=1, tiled=True),
    )
    inputs_here = lax.all_to_all(send_inputs, "expert", split_axis=0, concat_axis=0, tiled=True)
    projected_here, activation_here, results_here = expert_forward(inputs_here, full_in, full_down)
    results_home = lax.all_to_all(results_here, "expert", split_axis=0, concat_axis=0, tiled=True)
    grad_rows = lax.all_to_all(send_grads, "expert", split_axis=0, concat_axis=0, tiled=True)
    grad_hidden, grad_inputs = expert_backward(projected_here, grad_rows, full_in, full_down)
    inputs_back = lax.all_to_all(grad_inputs, "expert", split_axis=0, concat_axis=0, tiled=True)
    picked = results_home.reshape(experts * capacity, model_width)[slot_index].astype(jnp.float32)
    picked = picked.reshape(tok_rows, top_count, model_width)
    moe_out = jnp.sum(picked * gates[:, :, None], axis=1).astype(jnp.bfloat16)
    back_rows = inputs_back.reshape(experts * capacity, model_width)[slot_index].astype(jnp.float32)
    token_grad = jnp.sum(back_rows.reshape(tok_rows, top_count, model_width), axis=1).astype(
        jnp.bfloat16
    )
    column_part = inputs_here
    summed_in = lax.psum_scatter(
        (
            jnp.einsum(
                "sxcd,sxcj->dxj", column_part, grad_hidden, preferred_element_type=jnp.float32
            )
            * model_width ** (-0.5)
        ).astype(jnp.bfloat16),
        "dp",
        scatter_dimension=0,
        tiled=True,
    ).astype(jnp.float32)
    column_part = activation_here
    summed_down = lax.psum_scatter(
        (
            jnp.einsum("sxcf,sxcd->fxd", column_part, grad_rows, preferred_element_type=jnp.float32)
            * hidden_units ** (-0.5)
        ).astype(jnp.bfloat16),
        "dp",
        scatter_dimension=0,
        tiled=True,
    ).astype(jnp.float32)
    new_w_in = (w_in.astype(jnp.float32) - step_rate * jnp.transpose(summed_in, (1, 0, 2))).astype(
        jnp.bfloat16
    )
    new_w_down = (
        w_down.astype(jnp.float32) - step_rate * jnp.transpose(summed_down, (1, 0, 2))
    ).astype(jnp.bfloat16)
    return (moe_out, token_grad, new_w_in, new_w_down)


def solution(mesh):
    return jax.shard_map(
        body,
        mesh=mesh,
        in_specs=(
            P(("dp", "expert"), None),
            P(("dp", "expert"), None),
            P(("dp", "expert"), None),
            P("expert", "dp", None),
            P("expert", "dp", None),
            P(("dp", "expert"), None),
        ),
        out_specs=(
            P(("dp", "expert"), None),
            P(("dp", "expert"), None),
            P("expert", "dp", None),
            P("expert", "dp", None),
        ),
        check_vma=False,
    )
```

profile of v0, /device:TPU:25, one launch (start us, length us, event | category | flops | bytes accessed | tf_op | source)
XLA Modules:
  0.0 371.1 jit_solution(6107741425047522396)
XLA Ops:
  7.2 0.0 copy-start
  7.2 0.8 copy.34
  8.0 0.1 eq.29
  8.1 0.1 eq.25
  8.2 0.7 broadcast_multiply_fusion
  8.9 1.2 reduce-window.6
  10.1 0.2 slice_reduce_fusion
  10.4 0.1 fusion.51
  10.5 0.1 copy.33
  10.6 0.1 mul.160
  10.7 0.0 copy-done
  10.8 7.7 %scatter_custom_fusion = bf16[1024,1024]{1,0:T(8,128)(2,1)} fusion(s32[512]{0:T(512)S(1)} %bitcast.146, bf16[128,1024]{1,0:T(8,128)(2,1)S(1)} %copy-done, s32[1024]{0:T(1024)S(1)} %pad_clamp_fusion.1, bf16[]{:T(256)} %constant.17.clone.1), kind=kCustom, calls=%fused_computation.41 | custom fusion | bytes 2097154 | tf_op jit(solution)/shard_map/scatter | solution.py:68
  18.5 0.0 copy-start.5
  18.5 13.2 %all-to-all-start = ((bf16[32,1,32,1024]{3,2,1,0:T(8,128)(2,1)}), bf16[32,1,32,1024]{3,2,1,0:T(8,128)(2,1)S(1)}, u32[]{:S(2)}, u32[]{:S(2)}) async-start(bf16[32,1,32,1024]{3,2,1,0:T(8,128)(2,1)} %bitcast.4), calls=%async_computation | async-start | bytes 4194304 | tf_op jit(solution)/shard_map/all_to_all | solution.py:84
  31.7 0.0 copy-done.5
  31.7 0.1 copy.38
  31.8 0.1 mul.173
  31.9 0.0 copy-done.3
  32.0 7.8 %scatter_custom_fusion.1 = bf16[1024,1024]{1,0:T(8,128)(2,1)} fusion(s32[512]{0:T(512)S(1)} %bitcast.147, f32[512]{0:T(512)S(1)} %mul.173, bf16[]{:T(256)} %constant.17.clone.1, bf16[128,1024]{1,0:T(8,128)(2,1)S(1)} %copy-done.3, s32[1024]{0:T(1024)S(1)} %pad_clamp_fusion.1), kind=kCustom, calls=%fused_computation.40 | custom fusion | flops 1572864 | bytes 2365442 | tf_op jit(solution)/shard_map/scatter | solution.py:77
  39.8 40.7 %all-to-all-done = bf16[32,1,32,1024]{3,2,1,0:T(8,128)(2,1)S(1)} async-done(((bf16[32,1,32,1024]{3,2,1,0:T(8,128)(2,1)}), bf16[32,1,32,1024]{3,2,1,0:T(8,128)(2,1)S(1)}, u32[]{:S(2)}, u32[]{:S(2)}) %all-to-all-start) | async-done | bytes 2097184 | tf_op jit(solution)/shard_map/all_to_all | solution.py:84
  80.4 7.3 %all-to-all-start.2 = ((bf16[32,1,32,1024]{3,2,1,0:T(8,128)(2,1)}), bf16[32,1,32,1024]{3,2,1,0:T(8,128)(2,1)}, u32[]{:S(2)}, u32[]{:S(2)}) async-start(bf16[32,1,32,1024]{3,2,1,0:T(8,128)(2,1)} %bitcast.21), calls=%async_computation.2 | async-start | bytes 4194304 | tf_op jit(solution)/shard_map/all_to_all | solution.py:87
  87.7 0.0 all-gather.2.cloned.1.call-start
  87.8 0.7 all-gather.2.cloned.1.call-update
  88.4 0.0 copy-done.4
  88.4 18.9 %all_gather.7 = bf16[1,384,1024]{2,1,0:T(8,128)(2,1)S(1)} all-gather(bf16[1,24,1024]{2,1,0:T(8,128)(2,1)S(1)} %copy-done.4), channel_id=1, replica_groups=mesh['dp'=16,'expert'=32] {'dp'}, dimensions={1}, use_global_device_ids=true | all-gather | bytes 835584 | tf_op jit(solution)/shard_map/all_gather | solution.py:82
  107.4 26.6 %all-gather.2.cloned.1.call-done = bf16[1,1024,768]{2,1,0:T(8,128)(2,1)} async-done(((bf16[1,64,768]{2,1,0:T(8,128)(2,1)}), bf16[1,1024,768]{2,1,0:T(8,128)(2,1)}) %all-gather.2.cloned.1.call-update) | async-done | bytes 1572880 | tf_op jit(solution)/shard_map/all_gather | solution.py:81
  133.9 0.0 copy-done.1
  133.9 4.9 %multiply_bitcast_fusion = f32[32,1,32,768]{3,2,0,1:T(8,128)} fusion(bf16[32,1,32,1024]{3,2,1,0:T(8,128)(2,1)S(1)} %all-to-all-done, bf16[1,1024,768]{2,1,0:T(8,128)(2,1)} %all-gather.2.cloned.1.call-done), kind=kOutput, calls=%fused_computation.10 | convolution fusion | flops 1611399168 | bytes 6815744 | tf_op jit(solution)/shard_map/sxcd,xdj->sxcj/dot_general | solution.py:22
  138.9 0.0 all-to-all-done.2
  138.9 5.3 %fusion.44 = (bf16[32,32,384]{2,1,0:T(8,128)(2,1)S(1)}, bf16[32,32,384]{2,1,0:T(8,128)(2,1)S(1)}, bf16[32,32,384]{2,1,0:T(8,128)(2,1)}) fusion(f32[32,1,32,768]{3,2,0,1:T(8,128)} %multiply_bitcast_fusion, bf16[1,384,1024]{2,1,0:T(8,128)(2,1)S(1)} %all_gather.7, bf16[32,1,32,1024]{3,2,1,0:T(8,128)(2,1)} %all-to-all-done.2), kind=kOutput, calls=%fused_computation.50 | convolution fusion | flops 811597824 | bytes 8388608 | tf_op jit(solution)/shard_map/sxcd,xfd->sxcf/dot_general | solution.py:38
  144.2 0.9 copy-done.7
  145.1 0.2 copy-done.9
  145.4 0.0 copy-done.6
  145.4 3.2 fusion.14
  148.6 9.7 %all-to-all-start.3 = ((bf16[32,1,32,1024]{3,2,1,0:T(8,128)(2,1)}), bf16[32,1,32,1024]{3,2,1,0:T(8,128)(2,1)S(1)}, u32[]{:S(2)}, u32[]{:S(2)}) async-start(bf16[32,1,32,1024]{3,2,1,0:T(8,128)(2,1)} %fusion.14), calls=%async_computation.3 | async-start | bytes 4194304 | tf_op jit(solution)/shard_map/all_to_all | solution.py:89
  158.2 0.0 all-reduce.3.cloned.1.call-start
  158.3 3.9 %fusion.31 = bf16[384,1,1024]{0,2,1:T(8,128)(2,1)} fusion(bf16[32,32,384]{2,1,0:T(8,128)(2,1)} %get-tuple-element.18, bf16[32,1,32,1024]{3,2,1,0:T(8,128)(2,1)} %all-to-all-done.2), kind=kOutput, calls=%fused_computation.39 | convolution fusion | flops 806092800 | bytes 3670016 | tf_op jit(solution)/shard_map/sxcf,sxcd->fxd/dot_general | solution.py:112
  162.2 4.8 %copy.43 = bf16[384,1,1024]{2,1,0:T(2,128)(2,1)} copy(bf16[384,1,1024]{0,2,1:T(8,128)(2,1)} %fusion.31) | data formatting | bytes 1572864 | tf_op jit(solution)/shard_map/convert_element_type | solution.py:114
  167.0 0.0 all-reduce.3.cloned.1.call-update
  167.1 3.7 fusion.13
  170.8 36.4 %all-to-all-done.3 = bf16[32,1,32,1024]{3,2,1,0:T(8,128)(2,1)S(1)} async-done(((bf16[32,1,32,1024]{3,2,1,0:T(8,128)(2,1)}), bf16[32,1,32,1024]{3,2,1,0:T(8,128)(2,1)S(1)}, u32[]{:S(2)}, u32[]{:S(2)}) %all-to-all-start.3) | async-done | bytes 2097184 | tf_op jit(solution)/shard_map/all_to_all | solution.py:89
  207.1 7.6 %all-to-all-start.1 = ((bf16[32,1,32,1024]{3,2,1,0:T(8,128)(2,1)}), bf16[32,1,32,1024]{3,2,1,0:T(8,128)(2,1)}, u32[]{:S(2)}, u32[]{:S(2)}) async-start(bf16[32,1,32,1024]{3,2,1,0:T(8,128)(2,1)} %fusion.13), calls=%async_computation.1 | async-start | bytes 4194304 | tf_op jit(solution)/shard_map/all_to_all | solution.py:86
  214.8 0.0 reduce-scatter.4.cloned.1.call-start
  214.8 0.0 copy-done.8
  214.8 4.8 %fusion.23 = bf16[1024,768]{0,1:T(8,128)(2,1)} fusion(bf16[32,1,32,1024]{3,2,1,0:T(8,128)(2,1)} %copy-done.1, bf16[32,32,384]{2,1,0:T(8,128)(2,1)} %copy-done.9, bf16[32,32,384]{2,1,0:T(8,128)(2,1)S(1)} %copy-done.8), kind=kOutput, calls=%fused_computation.37 | convolution fusion | flops 1615331328 | bytes 5242880 | tf_op jit(solution)/shard_map/sxcd,sxcj->dxj/dot_general | solution.py:100
  219.7 2.6 copy.48
  222.3 0.0 reduce-scatter.4.cloned.1.call-update
  222.3 0.0 copy-done.2
  222.3 0.2 copy.41
  222.5 1.3 dynamic-slice
  224.5 62.4 %all-reduce.3.cloned.1.call-done = bf16[384,1,1024]{2,1,0:T(2,128)(2,1)} async-done(((bf16[384,1,1024]{2,1,0:T(2,128)(2,1)}), bf16[384,1,1024]{2,1,0:T(2,128)(2,1)}) %all-reduce.3.cloned.1.call-update) | async-done | bytes 786448
  286.8 1.0 fusion.49
  287.8 0.6 copy.45
  288.5 62.2 %reduce-scatter.4.cloned.1.call-done = bf16[64,768]{1,0:T(8,128)(2,1)} async-done(((bf16[1024,768]{1,0:T(8,128)(2,1)}), bf16[64,768]{1,0:T(8,128)(2,1)}) %reduce-scatter.4.cloned.1.call-update) | async-done | bytes 98320
  350.7 1.1 copy.49
  351.7 0.1 fusion.45
  351.8 0.8 copy.44
  352.6 2.0 gather_fusion.1
  354.6 0.4 gather.18
  355.1 2.1 reduce_sum.32
  357.2 0.0 all-to-all-done.1
  357.2 4.6 %gather_fusion = bf16[512,1024]{1,0:T(8,128)(2,1)S(1)} fusion(bf16[1024,1024]{1,0:T(8,128)(2,1)} %bitcast.20, s32[1024]{0:T(1024)S(1)} %pad_clamp_fusion), kind=kCustom, calls=%fused_computation.1 | custom fusion | bytes 2099200 | tf_op jit(solution)/shard_map/gather | solution.py:90
  361.8 0.7 reshape.219
  362.5 2.1 multiply_reduce_fusion
  (16 shorter events, 0.1 us)
Async XLA Ops:
  7.2 3.6 copy-start
  18.5 13.2 %copy-start.5 = (f32[128,4]{0,1:T(4,128)S(1)}, f32[128,4]{0,1:T(4,128)}, u32[]{:S(2)}) copy-start(f32[128,4]{0,1:T(4,128)} %param.8) | copy-start | bytes 6148
  18.5 13.4 %copy-start.3 = (bf16[128,1024]{1,0:T(8,128)(2,1)S(1)}, bf16[128,1024]{1,0:T(8,128)(2,1)}, u32[]{:S(2)}) copy-start(bf16[128,1024]{1,0:T(8,128)(2,1)} %param.11) | copy-start | bytes 786436
  18.5 61.9 %all-to-all-start = ((bf16[32,1,32,1024]{3,2,1,0:T(8,128)(2,1)}), bf16[32,1,32,1024]{3,2,1,0:T(8,128)(2,1)S(1)}, u32[]{:S(2)}, u32[]{:S(2)}) async-start(bf16[32,1,32,1024]{3,2,1,0:T(8,128)(2,1)} %bitcast.4), calls=%async_computation | async-start | bytes 4194304 | tf_op jit(solution)/shard_map/all_to_all | solution.py:84
  80.4 53.5 %copy-start.1 = (bf16[32,1,32,1024]{3,2,1,0:T(8,128)(2,1)}, bf16[32,1,32,1024]{3,2,1,0:T(8,128)(2,1)S(1)}, u32[]{:S(2)}) copy-start(bf16[32,1,32,1024]{3,2,1,0:T(8,128)(2,1)S(1)} %all-to-all-done) | copy-start | bytes 6291460
  80.4 8.0 %copy-start.4 = (bf16[1,24,1024]{2,1,0:T(8,128)(2,1)S(1)}, bf16[1,24,1024]{2,1,0:T(8,128)(2,1)}, u32[]{:S(2)}) copy-start(bf16[1,24,1024]{2,1,0:T(8,128)(2,1)} %param.10) | copy-start | bytes 147460
  80.4 58.4 %all-to-all-start.2 = ((bf16[32,1,32,1024]{3,2,1,0:T(8,128)(2,1)}), bf16[32,1,32,1024]{3,2,1,0:T(8,128)(2,1)}, u32[]{:S(2)}, u32[]{:S(2)}) async-start(bf16[32,1,32,1024]{3,2,1,0:T(8,128)(2,1)} %bitcast.21), calls=%async_computation.2 | async-start | bytes 4194304 | tf_op jit(solution)/shard_map/all_to_all | solution.py:87
  87.7 46.2 %all-gather.2.cloned.1.call-start = ((), (), s32[]{:S(2)}) async-start(), calls=%async_computation.5 | async-start | bytes 1671168 | tf_op jit(solution)/shard_map/all_gather | solution.py:81
  138.9 6.5 %copy-start.6 = (bf16[1,1024,768]{2,1,0:T(8,128)(2,1)S(1)}, bf16[1,1024,768]{2,1,0:T(8,128)(2,1)}, u32[]{:S(2)}) copy-start(bf16[1,1024,768]{2,1,0:T(8,128)(2,1)} %all-gather.2.cloned.1.call-done) | copy-start | bytes 4718596
  144.2 0.9 copy-start.7
  144.2 1.2 copy-start.9
  148.6 58.6 %all-to-all-start.3 = ((bf16[32,1,32,1024]{3,2,1,0:T(8,128)(2,1)}), bf16[32,1,32,1024]{3,2,1,0:T(8,128)(2,1)S(1)}, u32[]{:S(2)}, u32[]{:S(2)}) async-start(bf16[32,1,32,1024]{3,2,1,0:T(8,128)(2,1)} %fusion.14), calls=%async_computation.3 | async-start | bytes 4194304 | tf_op jit(solution)/shard_map/all_to_all | solution.py:89
  158.2 128.6 %all-reduce.3.cloned.1.call-start = ((), (), s32[]{:S(2)}) async-start(), calls=%async_computation.7 | async-start | bytes 3145728
  170.8 44.1 %copy-start.8 = (bf16[32,32,384]{2,1,0:T(8,128)(2,1)S(1)}, bf16[32,32,384]{2,1,0:T(8,128)(2,1)}, u32[]{:S(2)}) copy-start(bf16[32,32,384]{2,1,0:T(8,128)(2,1)} %copy-done.7) | copy-start | bytes 2359300
  207.1 150.0 %all-to-all-start.1 = ((bf16[32,1,32,1024]{3,2,1,0:T(8,128)(2,1)}), bf16[32,1,32,1024]{3,2,1,0:T(8,128)(2,1)}, u32[]{:S(2)}, u32[]{:S(2)}) async-start(bf16[32,1,32,1024]{3,2,1,0:T(8,128)(2,1)} %fusion.13), calls=%async_computation.1 | async-start | bytes 4194304 | tf_op jit(solution)/shard_map/all_to_all | solution.py:86
  214.8 135.9 %reduce-scatter.4.cloned.1.call-start = ((), (), s32[]{:S(2)}) async-start(), calls=%async_computation.6 | async-start | bytes 1671168
  219.7 2.7 copy-start.2
Sparse Core Ops, SparseCore 0:
  90.7 43.2 all-gather.1
  167.2 119.5 all-reduce.2
  289.9 60.7 reduce-scatter.3
where the time goes:
time: 372 us; the launch traced here: 371 us
  waiting for transfers between devices  229 us (62%)
  starting transfers between devices  37.9 us (10%)
  local copies, waits for them, and re-layouts  29.8 us (8%)
  matrix products  25.9 us (7%)
  blocking collectives  18.9 us (5%)
  other arithmetic  15.1 us (4%)
  between operations  14.6 us (4%)
    unnamed x5, waiting for transfers between devices  125 us
    all_to_all x1, waiting for transfers between devices, body(): lax.all_to_all(send_inputs, 'expert', split_axis=0, concat_axis=0, tiled=...  40.7 us
    all_to_all x1, waiting for transfers between devices, body(): lax.all_to_all(grad_inputs, 'expert', split_axis=0, concat_axis=0, tiled=...  36.4 us
    all_gather x1, waiting for transfers between devices, body(): lax.all_gather(w_in, 'dp', axis=1, tiled=True)  26.6 us
    all_gather x1, blocking collectives, body(): lax.all_gather(w_down, 'dp', axis=1, tiled=True)  18.9 us
    all_to_all x1, starting transfers between devices, body(): lax.all_to_all(send_inputs, 'expert', split_axis=0, concat_axis=0, tiled=...  13.2 us
    all_to_all x1, starting transfers between devices, body(): lax.all_to_all(grad_inputs, 'expert', split_axis=0, concat_axis=0, tiled=...  9.65 us
    unnamed x28, local copies, waits for them, and re-layouts  8.68 us
  transfers between devices with their start and end apart: 7, of which 5 were waited for; matrix products, arithmetic and copies ran while one was open for 11% of the time, Pallas kernels for 0%

commit v1 on v0

--- a/solution.py
+++ b/solution.py
@@ -2,6 +2,7 @@
 import jax.numpy as jnp
 from jax import lax
 from jax.sharding import PartitionSpec as P
+from jax.lax import axis_index, axis_size, ppermute
 
 step_rate = 0.5
 
@@ -77,8 +78,36 @@
         .set(scaled)
         .reshape(layout)
     )
+
+    def scan_node_for(own_rows, device_axis, where_dim=1):
+        ready, new, inter = (
+            axis_size(device_axis),
+            axis_index(device_axis),
+            own_rows.shape[where_dim],
+        )
+        fields = list(map(lambda no: (no, (no + 1) % ready), range(ready)))
+        in_order = list(map(lambda no: (no, (no - 1) % ready), range(ready)))
+        o_now = jnp.zeros(
+            (*own_rows.shape[:where_dim], ready * inter, *own_rows.shape[where_dim + 1 :]),
+            own_rows.dtype,
+        )
+        o_now = lax.dynamic_update_slice_in_dim(o_now, own_rows, new * inter, axis=where_dim)
+        main = all_rows = own_rows
+        r1 = ready // 2
+        for dev_i in range(1, r1 + 1):
+            main = ppermute(main, axis_name=device_axis, perm=fields)
+            o_now = lax.dynamic_update_slice_in_dim(
+                o_now, main, (new - dev_i) % ready * inter, axis=where_dim
+            )
+            if dev_i < ready - r1:
+                all_rows = ppermute(all_rows, axis_name=device_axis, perm=in_order)
+                o_now = lax.dynamic_update_slice_in_dim(
+                    o_now, all_rows, (new + dev_i) % ready * inter, axis=where_dim
+                )
+        return o_now
+
     full_in, full_down = (
-        lax.all_gather(w_in, "dp", axis=1, tiled=True),
+        scan_node_for(w_in, "dp"),
         lax.all_gather(w_down, "dp", axis=1, tiled=True),
     )
     inputs_here = lax.all_to_all(send_inputs, "expert", split_axis=0, concat_axis=0, tiled=True)

time: 372 us -> 371 us (level)
  waiting for transfers between devices: 229 us -> 190 us
  starting transfers between devices: 37.9 us -> 60 us
  local copies, waits for them, and re-layouts: 29.8 us -> 42.8 us
    all_to_all x1, waiting for transfers between devices: 40.7 us -> 13 us  [body(): lax.all_to_all(send_inputs, 'expert', split_axis=0, concat_axis=0, tiled=...]
    all_gather x1 -> x0, waiting for transfers between devices: 26.6 us -> none  [body(): lax.all_gather(w_in, 'dp', axis=1, tiled=True)]
    ppermute x0 -> x15, starting transfers between devices: none -> 24.9 us  [the longest x8 24.9 us: scan_node_for(): main = ppermute(main, axis_name=device_axis, perm=fields)]
    dynamic_update_slice x0 -> x16, local copies, waits for them, and re-layouts: none -> 13 us  [the longest x8 6.97 us: scan_node_for(): lax.dynamic_update_slice_in_dim(o_now, main, (new - dev_i) % ready * inte...]
    all_to_all x1, waiting for transfers between devices: 0.01 us -> 9.23 us  [body(): lax.all_to_all(send_grads, 'expert', split_axis=0, concat_axis=0, tiled=T...]
    unnamed x5 -> x4, waiting for transfers between devices: 125 us -> 128 us
    unnamed x28 -> x24, local copies, waits for them, and re-layouts: 8.68 us -> 7.5 us
  transfers between devices with their start and end apart: 7 -> 21, of which waited for: 5 -> 10; matrix products, arithmetic and copies ran while one was open for 11% -> 16% of each run, Pallas kernels for 0% -> 0%
where the time goes in v1:
time: 371 us; the launch traced here: 370 us
  waiting for transfers between devices  190 us (51%)
  starting transfers between devices  60 us (16%)
  local copies, waits for them, and re-layouts  42.8 us (12%)
  matrix products  27.8 us (7%)
  blocking collectives  18.4 us (5%)
  other arithmetic  15.9 us (4%)
  between operations  15 us (4%)
    unnamed x4, waiting for transfers between devices  128 us
    all_to_all x1, waiting for transfers between devices, body(): lax.all_to_all(grad_inputs, 'expert', split_axis=0, concat_axis=0, tiled=...  36.1 us
    ppermute x8, starting transfers between devices, scan_node_for(): main = ppermute(main, axis_name=device_axis, perm=fields)  24.9 us
    all_gather x1, blocking collectives, body(): lax.all_gather(w_down, 'dp', axis=1, tiled=True)  18.4 us
    all_to_all x1, starting transfers between devices, body(): lax.all_to_all(send_inputs, 'expert', split_axis=0, concat_axis=0, tiled=...  13 us
    all_to_all x1, waiting for transfers between devices, body(): lax.all_to_all(send_inputs, 'expert', split_axis=0, concat_axis=0, tiled=...  13 us
    all_to_all x1, waiting for transfers between devices, body(): lax.all_to_all(send_grads, 'expert', split_axis=0, concat_axis=0, tiled=T...  9.23 us
    scatter x1, other arithmetic, body(): send_grads = jnp.zeros((experts * capacity, model_width), jnp.bfloat16).a...  8.61 us
  transfers between devices with their start and end apart: 21, of which 10 were waited for; matrix products, arithmetic and copies ran while one was open for 16% of the time, Pallas kernels for 0%

profile of v1, /device:TPU:25, one launch (start us, length us, event | category | flops | bytes accessed | tf_op | source)
XLA Modules:
  0.0 370.2 jit_solution(11377547816620565146)
XLA Ops:
  7.2 0.8 copy.34
  8.2 0.7 broadcast_multiply_fusion
  8.9 1.2 reduce-window.6
  10.7 7.7 %scatter_custom_fusion = bf16[1024,1024]{1,0:T(8,128)(2,1)} fusion(s32[512]{0:T(512)S(1)} %bitcast.173, bf16[128,1024]{1,0:T(8,128)(2,1)S(1)} %copy-done, s32[1024]{0:T(1024)S(1)} %pad_clamp_fusion.1, bf16[]{:T(256)} %constant.143.clone.1), kind=kCustom, calls=%fused_computation.41 | custom fusion | bytes 2097154 | tf_op jit(solution)/shard_map/scatter | solution.py:69
  18.5 13.0 %all-to-all-start = ((bf16[32,1,32,1024]{3,2,1,0:T(8,128)(2,1)}), bf16[32,1,32,1024]{3,2,1,0:T(8,128)(2,1)S(1)}, u32[]{:S(2)}, u32[]{:S(2)}) async-start(bf16[32,1,32,1024]{3,2,1,0:T(8,128)(2,1)} %bitcast.21), calls=%async_computation | async-start | bytes 4194304 | tf_op jit(solution)/shard_map/all_to_all | solution.py:113
  31.5 3.4 collective-permute-start
  34.9 18.4 %all_gather.3 = bf16[1,384,1024]{2,1,0:T(8,128)(2,1)S(1)} all-gather(bf16[1,24,1024]{2,1,0:T(8,128)(2,1)S(1)} %copy-done.3), channel_id=1, replica_groups=mesh['dp'=16,'expert'=32] {'dp'}, dimensions={1}, use_global_device_ids=true | all-gather | bytes 835584 | tf_op jit(solution)/shard_map/all_gather | solution.py:111
  53.3 1.3 broadcast.193
  54.6 0.6 bitcast_dynamic-update-slice_fusion.15
  55.5 8.6 %scatter_custom_fusion.1 = bf16[1024,1024]{1,0:T(8,128)(2,1)} fusion(s32[512]{0:T(512)S(1)} %bitcast.174, f32[512]{0:T(512)S(1)} %mul.232, bf16[]{:T(256)} %constant.143.clone.1, bf16[128,1024]{1,0:T(8,128)(2,1)} %param.11, s32[1024]{0:T(1024)S(1)} %pad_clamp_fusion.1), kind=kCustom, calls=%fused_computation.40 | custom fusion | flops 1572864 | bytes 2365442 | tf_op jit(solution)/shard_map/scatter | solution.py:78
  64.1 1.7 collective-permute-start.2
  65.9 1.6 bitcast_dynamic-update-slice_fusion.14
  67.4 13.0 %all-to-all-done = bf16[32,1,32,1024]{3,2,1,0:T(8,128)(2,1)S(1)} async-done(((bf16[32,1,32,1024]{3,2,1,0:T(8,128)(2,1)}), bf16[32,1,32,1024]{3,2,1,0:T(8,128)(2,1)S(1)}, u32[]{:S(2)}, u32[]{:S(2)}) %all-to-all-start) | async-done | bytes 2097184 | tf_op jit(solution)/shard_map/all_to_all | solution.py:113
  80.4 7.4 %all-to-all-start.2 = ((bf16[32,1,32,1024]{3,2,1,0:T(8,128)(2,1)}), bf16[32,1,32,1024]{3,2,1,0:T(8,128)(2,1)}, u32[]{:S(2)}, u32[]{:S(2)}) async-start(bf16[32,1,32,1024]{3,2,1,0:T(8,128)(2,1)} %bitcast.34), calls=%async_computation.2 | async-start | bytes 4194304 | tf_op jit(solution)/shard_map/all_to_all | solution.py:116
  87.8 0.6 bitcast_dynamic-update-slice_fusion.13
  88.4 3.6 collective-permute-start.4
  92.0 1.6 bitcast_dynamic-update-slice_fusion.12
  93.6 1.5 bitcast_dynamic-update-slice_fusion.11
  95.1 2.9 collective-permute-start.6
  98.1 0.6 bitcast_dynamic-update-slice_fusion.10
  98.7 0.6 bitcast_dynamic-update-slice_fusion.9
  99.3 0.4 collective-permute-done.6
  99.7 3.6 collective-permute-start.8
  103.3 0.4 collective-permute-done.7
  103.7 0.6 bitcast_dynamic-update-slice_fusion.8
  104.3 0.6 bitcast_dynamic-update-slice_fusion.7
  105.0 3.6 collective-permute-start.10
  108.6 0.8 collective-permute-done.9
  109.4 0.6 bitcast_dynamic-update-slice_fusion.6
  110.0 0.6 bitcast_dynamic-update-slice_fusion.5
  110.6 3.2 collective-permute-start.12
  113.8 1.2 collective-permute-done.11
  115.0 0.6 bitcast_dynamic-update-slice_fusion.4
  115.7 0.6 bitcast_dynamic-update-slice_fusion.3
  116.3 3.0 collective-permute-start.14
  119.3 0.6 bitcast_dynamic-update-slice_fusion.2
  119.9 0.8 collective-permute-done.13
  120.7 0.6 bitcast_dynamic-update-slice_fusion.1
  121.3 0.7 bitcast_dynamic-update-slice_fusion
  122.0 5.0 %multiply_bitcast_fusion = f32[32,1,32,768]{3,2,0,1:T(8,128)} fusion(bf16[32,1,32,1024]{3,2,1,0:T(8,128)(2,1)S(1)} %all-to-all-done, bf16[1024,768]{1,0:T(8,128)(2,1)} %bitcast_dynamic-update-slice_fusion), kind=kOutput, calls=%fused_computation.10 | convolution fusion | flops 1611399168 | bytes 6815744 | tf_op jit(solution)/shard_map/sxcd,xdj->sxcj/dot_general | solution.py:23
  126.9 9.2 %all-to-all-done.2 = bf16[32,1,32,1024]{3,2,1,0:T(8,128)(2,1)} async-done(((bf16[32,1,32,1024]{3,2,1,0:T(8,128)(2,1)}), bf16[32,1,32,1024]{3,2,1,0:T(8,128)(2,1)}, u32[]{:S(2)}, u32[]{:S(2)}) %all-to-all-start.2) | async-done | bytes 2097184 | tf_op jit(solution)/shard_map/all_to_all | solution.py:116
  136.2 5.2 %fusion.44 = (bf16[32,32,384]{2,1,0:T(8,128)(2,1)S(1)}, bf16[32,32,384]{2,1,0:T(8,128)(2,1)S(1)}, bf16[32,32,384]{2,1,0:T(8,128)(2,1)}) fusion(f32[32,1,32,768]{3,2,0,1:T(8,128)} %multiply_bitcast_fusion, bf16[1,384,1024]{2,1,0:T(8,128)(2,1)S(1)} %all_gather.3, bf16[32,1,32,1024]{3,2,1,0:T(8,128)(2,1)} %all-to-all-done.2), kind=kOutput, calls=%fused_computation.50 | convolution fusion | flops 811597824 | bytes 8388608 | tf_op jit(solution)/shard_map/sxcd,xfd->sxcf/dot_general | solution.py:39
  141.4 5.2 %fusion.1 = bf16[32,1,32,1024]{3,2,1,0:T(8,128)(2,1)} fusion(bf16[1024,768]{1,0:T(8,128)(2,1)} %bitcast_dynamic-update-slice_fusion, bf16[32,32,384]{2,1,0:T(8,128)(2,1)S(1)} %get-tuple-element.17, bf16[32,32,384]{2,1,0:T(8,128)(2,1)S(1)} %get-tuple-element.16), kind=kOutput, calls=%fused_computation.11 | convolution fusion | flops 1615855616 | bytes 5242880 | tf_op jit(solution)/shard_map/sxcj,xdj->sxcd/dot_general | solution.py:49
  146.6 7.1 %all-to-all-start.3 = ((bf16[32,1,32,1024]{3,2,1,0:T(8,128)(2,1)}), bf16[32,1,32,1024]{3,2,1,0:T(8,128)(2,1)S(1)}, u32[]{:S(2)}, u32[]{:S(2)}) async-start(bf16[32,1,32,1024]{3,2,1,0:T(8,128)(2,1)} %fusion.1), calls=%async_computation.3 | async-start | bytes 4194304 | tf_op jit(solution)/shard_map/all_to_all | solution.py:118
  153.7 3.9 %fusion.31 = bf16[384,1,1024]{0,2,1:T(8,128)(2,1)} fusion(bf16[32,32,384]{2,1,0:T(8,128)(2,1)} %get-tuple-element.18, bf16[32,1,32,1024]{3,2,1,0:T(8,128)(2,1)} %all-to-all-done.2), kind=kOutput, calls=%fused_computation.39 | convolution fusion | flops 806092800 | bytes 3670016 | tf_op jit(solution)/shard_map/sxcf,sxcd->fxd/dot_general | solution.py:141
  157.7 4.8 %copy.43 = bf16[384,1,1024]{2,1,0:T(2,128)(2,1)} copy(bf16[384,1,1024]{0,2,1:T(8,128)(2,1)} %fusion.31) | data formatting | bytes 1572864 | tf_op jit(solution)/shard_map/convert_element_type | solution.py:143
  162.5 3.7 %fusion.14 = bf16[32,1,32,1024]{3,2,1,0:T(8,128)(2,1)} fusion(bf16[32,32,384]{2,1,0:T(8,128)(2,1)} %get-tuple-element.18, bf16[1,384,1024]{2,1,0:T(8,128)(2,1)S(1)} %all_gather.3), kind=kOutput, calls=%fused_computation.22 | convolution fusion | flops 807403520 | bytes 3670016 | tf_op jit(solution)/shard_map/sxcf,xfd->sxcd/dot_general | solution.py:30
  166.2 36.1 %all-to-all-done.3 = bf16[32,1,32,1024]{3,2,1,0:T(8,128)(2,1)S(1)} async-done(((bf16[32,1,32,1024]{3,2,1,0:T(8,128)(2,1)}), bf16[32,1,32,1024]{3,2,1,0:T(8,128)(2,1)S(1)}, u32[]{:S(2)}, u32[]{:S(2)}) %all-to-all-start.3) | async-done | bytes 2097184 | tf_op jit(solution)/shard_map/all_to_all | solution.py:118
  202.3 7.2 %all-to-all-start.1 = ((bf16[32,1,32,1024]{3,2,1,0:T(8,128)(2,1)}), bf16[32,1,32,1024]{3,2,1,0:T(8,128)(2,1)}, u32[]{:S(2)}, u32[]{:S(2)}) async-start(bf16[32,1,32,1024]{3,2,1,0:T(8,128)(2,1)} %fusion.14), calls=%async_computation.1 | async-start | bytes 4194304 | tf_op jit(solution)/shard_map/all_to_all | solution.py:115
  209.9 4.8 %fusion.23 = bf16[1024,768]{0,1:T(8,128)(2,1)} fusion(bf16[32,1,32,1024]{3,2,1,0:T(8,128)(2,1)} %copy-done.1, bf16[32,32,384]{2,1,0:T(8,128)(2,1)} %copy-done.7, bf16[32,32,384]{2,1,0:T(8,128)(2,1)S(1)} %copy-done.6), kind=kOutput, calls=%fused_computation.37 | convolution fusion | flops 1615331328 | bytes 5242880 | tf_op jit(solution)/shard_map/sxcd,sxcj->dxj/dot_general | solution.py:129
  214.7 2.6 copy.48
  217.5 1.3 dynamic-slice
  219.4 66.2 %all-reduce.3.cloned.1.call-done = bf16[384,1,1024]{2,1,0:T(2,128)(2,1)} async-done(((bf16[384,1,1024]{2,1,0:T(2,128)(2,1)}), bf16[384,1,1024]{2,1,0:T(2,128)(2,1)}) %all-reduce.3.cloned.1.call-update) | async-done | bytes 786448
  285.6 1.0 fusion.49
  286.7 0.6 copy.45
  287.3 62.2 %reduce-scatter.4.cloned.1.call-done = bf16[64,768]{1,0:T(8,128)(2,1)} async-done(((bf16[1024,768]{1,0:T(8,128)(2,1)}), bf16[64,768]{1,0:T(8,128)(2,1)}) %reduce-scatter.4.cloned.1.call-update) | async-done | bytes 98320
  349.5 1.1 copy.49
  350.6 0.8 copy.44
  351.4 2.0 gather_fusion.1
  353.5 0.4 gather.18
  353.9 2.1 reduce_sum.32
  356.0 4.6 %gather_fusion = bf16[512,1024]{1,0:T(8,128)(2,1)S(1)} fusion(bf16[1024,1024]{1,0:T(8,128)(2,1)} %bitcast.33, s32[1024]{0:T(1024)S(1)} %pad_clamp_fusion), kind=kCustom, calls=%fused_computation.1 | custom fusion | bytes 2099200 | tf_op jit(solution)/shard_map/gather | solution.py:119
  360.6 0.7 reshape.296
  361.3 2.1 multiply_reduce_fusion
  (55 shorter events, 1.7 us)
Async XLA Ops:
  7.2 3.6 copy-start
  18.5 13.0 %copy-start.2 = (bf16[1,64,768]{2,1,0:T(8,128)(2,1)S(1)}, bf16[1,64,768]{2,1,0:T(8,128)(2,1)}, u32[]{:S(2)}) copy-start(bf16[1,64,768]{2,1,0:T(8,128)(2,1)} %param.9) | copy-start | bytes 294916
  18.5 16.4 %copy-start.3 = (bf16[1,24,1024]{2,1,0:T(8,128)(2,1)S(1)}, bf16[1,24,1024]{2,1,0:T(8,128)(2,1)}, u32[]{:S(2)}) copy-start(bf16[1,24,1024]{2,1,0:T(8,128)(2,1)} %param.10) | copy-start | bytes 147460
  18.5 61.9 %all-to-all-start = ((bf16[32,1,32,1024]{3,2,1,0:T(8,128)(2,1)}), bf16[32,1,32,1024]{3,2,1,0:T(8,128)(2,1)S(1)}, u32[]{:S(2)}, u32[]{:S(2)}) async-start(bf16[32,1,32,1024]{3,2,1,0:T(8,128)(2,1)} %bitcast.21), calls=%async_computation | async-start | bytes 4194304 | tf_op jit(solution)/shard_map/all_to_all | solution.py:113
  31.5 23.7 %copy-start.4 = (f32[128,4]{0,1:T(4,128)S(1)}, f32[128,4]{0,1:T(4,128)}, u32[]{:S(2)}) copy-start(f32[128,4]{0,1:T(4,128)} %param.8) | copy-start | bytes 6148
  31.5 32.6 %collective-permute-start = (bf16[1,64,768]{2,1,0:T(8,128)(2,1)S(1)}, bf16[1,64,768]{2,1,0:T(8,128)(2,1)}, u32[]{:S(2)}, u32[]{:S(2)}) collective-permute-start(bf16[1,64,768]{2,1,0:T(8,128)(2,1)S(1)} %copy-done.2), channel_id=1, source_target_pairs={{0,32},{32,64},{64,96},{96,128},{128,160},{160,192},{192,224},{224... | collective-permute-start | bytes 294920 | tf_op jit(solution)/shard_map/ppermute | solution.py:98
  34.9 31.0 %collective-permute-start.1 = (bf16[1,64,768]{2,1,0:T(8,128)(2,1)S(1)}, bf16[1,64,768]{2,1,0:T(8,128)(2,1)S(1)}, u32[]{:S(2)}, u32[]{:S(2)}) collective-permute-start(bf16[1,64,768]{2,1,0:T(8,128)(2,1)S(1)} %copy-done.2), channel_id=1, source_target_pairs={{0,480},{32,0},{64,32},{96,64},{128,96},{160,128},{192,160},{224,1... | collective-permute-start | bytes 294920 | tf_op jit(solution)/shard_map/ppermute | solution.py:103
  64.1 24.3 %collective-permute-start.2 = (bf16[1,64,768]{2,1,0:T(8,128)(2,1)}, bf16[1,64,768]{2,1,0:T(8,128)(2,1)}, u32[]{:S(2)}, u32[]{:S(2)}) collective-permute-start(bf16[1,64,768]{2,1,0:T(8,128)(2,1)} %collective-permute-done), channel_id=1, source_target_pairs={{0,32},{32,64},{64,96},{96,128},{128,160},{160,192},{192,224},{224... | collective-permute-start | bytes 294920 | tf_op jit(solution)/shard_map/ppermute | solution.py:98
  65.9 26.2 %collective-permute-start.3 = (bf16[1,64,768]{2,1,0:T(8,128)(2,1)S(1)}, bf16[1,64,768]{2,1,0:T(8,128)(2,1)}, u32[]{:S(2)}, u32[]{:S(2)}) collective-permute-start(bf16[1,64,768]{2,1,0:T(8,128)(2,1)S(1)} %collective-permute-done.1), channel_id=1, source_target_pairs={{0,480},{32,0},{64,32},{96,64},{128,96},{160,128},{192,160},{224,1... | collective-permute-start | bytes 294920 | tf_op jit(solution)/shard_map/ppermute | solution.py:103
  80.4 41.6 %copy-start.1 = (bf16[32,1,32,1024]{3,2,1,0:T(8,128)(2,1)}, bf16[32,1,32,1024]{3,2,1,0:T(8,128)(2,1)S(1)}, u32[]{:S(2)}) copy-start(bf16[32,1,32,1024]{3,2,1,0:T(8,128)(2,1)S(1)} %all-to-all-done) | copy-start | bytes 6291460
  80.4 55.8 %all-to-all-start.2 = ((bf16[32,1,32,1024]{3,2,1,0:T(8,128)(2,1)}), bf16[32,1,32,1024]{3,2,1,0:T(8,128)(2,1)}, u32[]{:S(2)}, u32[]{:S(2)}) async-start(bf16[32,1,32,1024]{3,2,1,0:T(8,128)(2,1)} %bitcast.34), calls=%async_computation.2 | async-start | bytes 4194304 | tf_op jit(solution)/shard_map/all_to_all | solution.py:116
  88.4 6.7 %collective-permute-start.4 = (bf16[1,64,768]{2,1,0:T(8,128)(2,1)}, bf16[1,64,768]{2,1,0:T(8,128)(2,1)S(1)}, u32[]{:S(2)}, u32[]{:S(2)}) collective-permute-start(bf16[1,64,768]{2,1,0:T(8,128)(2,1)} %collective-permute-done.2), channel_id=1, source_target_pairs={{0,32},{32,64},{64,96},{96,128},{128,160},{160,192},{192,224},{224... | collective-permute-start | bytes 294920 | tf_op jit(solution)/shard_map/ppermute | solution.py:98
  92.0 6.0 %collective-permute-start.5 = (bf16[1,64,768]{2,1,0:T(8,128)(2,1)}, bf16[1,64,768]{2,1,0:T(8,128)(2,1)S(1)}, u32[]{:S(2)}, u32[]{:S(2)}) collective-permute-start(bf16[1,64,768]{2,1,0:T(8,128)(2,1)} %collective-permute-done.3), channel_id=1, source_target_pairs={{0,480},{32,0},{64,32},{96,64},{128,96},{160,128},{192,160},{224,1... | collective-permute-start | bytes 294920 | tf_op jit(solution)/shard_map/ppermute | solution.py:103
  95.1 4.6 %collective-permute-start.6 = (bf16[1,64,768]{2,1,0:T(8,128)(2,1)S(1)}, bf16[1,64,768]{2,1,0:T(8,128)(2,1)S(1)}, u32[]{:S(2)}, u32[]{:S(2)}) collective-permute-start(bf16[1,64,768]{2,1,0:T(8,128)(2,1)S(1)} %collective-permute-done.4), channel_id=1, source_target_pairs={{0,32},{32,64},{64,96},{96,128},{128,160},{160,192},{192,224},{224... | collective-permute-start | bytes 294920 | tf_op jit(solution)/shard_map/ppermute | solution.py:98
  98.1 5.7 %collective-permute-start.7 = (bf16[1,64,768]{2,1,0:T(8,128)(2,1)S(1)}, bf16[1,64,768]{2,1,0:T(8,128)(2,1)S(1)}, u32[]{:S(2)}, u32[]{:S(2)}) collective-permute-start(bf16[1,64,768]{2,1,0:T(8,128)(2,1)S(1)} %collective-permute-done.5), channel_id=1, source_target_pairs={{0,480},{32,0},{64,32},{96,64},{128,96},{160,128},{192,160},{224,1... | collective-permute-start | bytes 294920 | tf_op jit(solution)/shard_map/ppermute | solution.py:103
  99.7 5.3 %collective-permute-start.8 = (bf16[1,64,768]{2,1,0:T(8,128)(2,1)S(1)}, bf16[1,64,768]{2,1,0:T(8,128)(2,1)S(1)}, u32[]{:S(2)}, u32[]{:S(2)}) collective-permute-start(bf16[1,64,768]{2,1,0:T(8,128)(2,1)S(1)} %collective-permute-done.6), channel_id=1, source_target_pairs={{0,32},{32,64},{64,96},{96,128},{128,160},{160,192},{192,224},{224... | collective-permute-start | bytes 294920 | tf_op jit(solution)/shard_map/ppermute | solution.py:98
  103.7 5.7 %collective-permute-start.9 = (bf16[1,64,768]{2,1,0:T(8,128)(2,1)S(1)}, bf16[1,64,768]{2,1,0:T(8,128)(2,1)S(1)}, u32[]{:S(2)}, u32[]{:S(2)}) collective-permute-start(bf16[1,64,768]{2,1,0:T(8,128)(2,1)S(1)} %collective-permute-done.7), channel_id=1, source_target_pairs={{0,480},{32,0},{64,32},{96,64},{128,96},{160,128},{192,160},{224,1... | collective-permute-start | bytes 294920 | tf_op jit(solution)/shard_map/ppermute | solution.py:103
  105.0 5.7 %collective-permute-start.10 = (bf16[1,64,768]{2,1,0:T(8,128)(2,1)S(1)}, bf16[1,64,768]{2,1,0:T(8,128)(2,1)S(1)}, u32[]{:S(2)}, u32[]{:S(2)}) collective-permute-start(bf16[1,64,768]{2,1,0:T(8,128)(2,1)S(1)} %collective-permute-done.8), channel_id=1, source_target_pairs={{0,32},{32,64},{64,96},{96,128},{128,160},{160,192},{192,224},{224... | collective-permute-start | bytes 294920 | tf_op jit(solution)/shard_map/ppermute | solution.py:98
  109.4 5.7 %collective-permute-start.11 = (bf16[1,64,768]{2,1,0:T(8,128)(2,1)S(1)}, bf16[1,64,768]{2,1,0:T(8,128)(2,1)S(1)}, u32[]{:S(2)}, u32[]{:S(2)}) collective-permute-start(bf16[1,64,768]{2,1,0:T(8,128)(2,1)S(1)} %collective-permute-done.9), channel_id=1, source_target_pairs={{0,480},{32,0},{64,32},{96,64},{128,96},{160,128},{192,160},{224,1... | collective-permute-start | bytes 294920 | tf_op jit(solution)/shard_map/ppermute | solution.py:103
  110.6 5.7 %collective-permute-start.12 = (bf16[1,64,768]{2,1,0:T(8,128)(2,1)S(1)}, bf16[1,64,768]{2,1,0:T(8,128)(2,1)S(1)}, u32[]{:S(2)}, u32[]{:S(2)}) collective-permute-start(bf16[1,64,768]{2,1,0:T(8,128)(2,1)S(1)} %collective-permute-done.10), channel_id=1, source_target_pairs={{0,32},{32,64},{64,96},{96,128},{128,160},{160,192},{192,224},{224... | collective-permute-start | bytes 294920 | tf_op jit(solution)/shard_map/ppermute | solution.py:98
  115.0 5.7 %collective-permute-start.13 = (bf16[1,64,768]{2,1,0:T(8,128)(2,1)S(1)}, bf16[1,64,768]{2,1,0:T(8,128)(2,1)S(1)}, u32[]{:S(2)}, u32[]{:S(2)}) collective-permute-start(bf16[1,64,768]{2,1,0:T(8,128)(2,1)S(1)} %collective-permute-done.11), channel_id=1, source_target_pairs={{0,480},{32,0},{64,32},{96,64},{128,96},{160,128},{192,160},{224,1... | collective-permute-start | bytes 294920 | tf_op jit(solution)/shard_map/ppermute | solution.py:103
  116.3 5.0 %collective-permute-start.14 = (bf16[1,64,768]{2,1,0:T(8,128)(2,1)S(1)}, bf16[1,64,768]{2,1,0:T(8,128)(2,1)S(1)}, u32[]{:S(2)}, u32[]{:S(2)}) collective-permute-start(bf16[1,64,768]{2,1,0:T(8,128)(2,1)S(1)} %collective-permute-done.12), channel_id=1, source_target_pairs={{0,32},{32,64},{64,96},{96,128},{128,160},{160,192},{192,224},{224... | collective-permute-start | bytes 294920 | tf_op jit(solution)/shard_map/ppermute | solution.py:98
  141.4 5.2 %copy-start.5 = (bf16[32,32,384]{2,1,0:T(8,128)(2,1)}, bf16[32,32,384]{2,1,0:T(8,128)(2,1)S(1)}, u32[]{:S(2)}) copy-start(bf16[32,32,384]{2,1,0:T(8,128)(2,1)S(1)} %get-tuple-element.16) | copy-start | bytes 2359300
  141.4 5.2 %copy-start.7 = (bf16[32,32,384]{2,1,0:T(8,128)(2,1)}, bf16[32,32,384]{2,1,0:T(8,128)(2,1)S(1)}, u32[]{:S(2)}) copy-start(bf16[32,32,384]{2,1,0:T(8,128)(2,1)S(1)} %get-tuple-element.17) | copy-start | bytes 2359300
  146.6 55.7 %all-to-all-start.3 = ((bf16[32,1,32,1024]{3,2,1,0:T(8,128)(2,1)}), bf16[32,1,32,1024]{3,2,1,0:T(8,128)(2,1)S(1)}, u32[]{:S(2)}, u32[]{:S(2)}) async-start(bf16[32,1,32,1024]{3,2,1,0:T(8,128)(2,1)} %fusion.1), calls=%async_computation.3 | async-start | bytes 4194304 | tf_op jit(solution)/shard_map/all_to_all | solution.py:118
  153.7 132.0 %all-reduce.3.cloned.1.call-start = ((), (), s32[]{:S(2)}) async-start(), calls=%async_computation.6 | async-start | bytes 3145728
  166.2 43.7 %copy-start.6 = (bf16[32,32,384]{2,1,0:T(8,128)(2,1)S(1)}, bf16[32,32,384]{2,1,0:T(8,128)(2,1)}, u32[]{:S(2)}) copy-start(bf16[32,32,384]{2,1,0:T(8,128)(2,1)} %copy-done.5) | copy-start | bytes 2359300
  202.3 153.7 %all-to-all-start.1 = ((bf16[32,1,32,1024]{3,2,1,0:T(8,128)(2,1)}), bf16[32,1,32,1024]{3,2,1,0:T(8,128)(2,1)}, u32[]{:S(2)}, u32[]{:S(2)}) async-start(bf16[32,1,32,1024]{3,2,1,0:T(8,128)(2,1)} %fusion.14), calls=%async_computation.1 | async-start | bytes 4194304 | tf_op jit(solution)/shard_map/all_to_all | solution.py:115
  209.5 140.0 %reduce-scatter.4.cloned.1.call-start = ((), (), s32[]{:S(2)}) async-start(), calls=%async_computation.5 | async-start | bytes 1671168
Sparse Core Ops, SparseCore 0:
  162.6 122.9 all-reduce.2
  288.7 60.7 reduce-scatter.3
